TPU v7x, 32 devices: a whole 2x2x4 slice. The times are simulated.
32 devices in a mesh: row: 8 (over z, core), col: 4 (over y, x).
Axes of the slice: x: 2, y: 2, z: 4, core: 2. Of those that a mesh axis runs over, the one named last changes fastest.
Arguments:
- activations: bfloat16 [1024, 8192], P('col', 'row'), may hold values from -6 to 6
- out_grad: bfloat16 [1024, 8192], P('col', 'row'), may hold values from -6 to 6
- gate_pre: bfloat16 [1024, 16384], P('row', 'col'), may hold values from -8 to 8
- up_proj: bfloat16 [1024, 16384], P('row', 'col'), may hold values from -6 to 6
- gate_weight: bfloat16 [8192, 16384], P('row', 'col'), may hold values from -0.0625 to 0.0625
- up_weight: bfloat16 [8192, 16384], P('row', 'col'), may hold values from -0.0625 to 0.0625
- down_weight: bfloat16 [16384, 8192], P('col', 'row'), may hold values from -0.046875 to 0.046875
Outputs:
- input_grad: bfloat16 [1024, 8192], P('col', 'row')
- gate_grad: bfloat16 [8192, 16384], P('row', 'col')
- up_grad: bfloat16 [8192, 16384], P('row', 'col')
- down_grad: bfloat16 [16384, 8192], P('col', 'row')
All inputs are finite; a program needn't handle non-finite values.
Results may differ from a plain program's by a relative error of at most 0.0051.
Values may be sent and summed in bfloat16 or wider, within the bound.
No kernel may reach another device: no remote copies, remote signals or barrier semaphores. Data moves between devices by JAX's collectives and lax.ppermute only.
A program may use at most 192 MiB of HBM per device.

v0:
```python
import jax
import jax.numpy as jnp
from jax import lax
from jax.sharding import PartitionSpec as P

CONTRACT_LAST = (((1,), (1,)), ((), ()))
CONTRACT_FIRST = (((0,), (0,)), ((), ()))
ROW = ("z", "core")


def shift_perm(n, s):
    return [(i, (i + s) % n) for i in range(n)]


def gather_col(block):
    n = lax.axis_size("col")
    c = lax.axis_index("col")
    rows = block.shape[0]
    full = jnp.zeros((n * rows,) + block.shape[1:], block.dtype)
    full = lax.dynamic_update_slice_in_dim(full, block, c * rows, axis=0)
    for s in range(1, n):
        part = lax.ppermute(block, "col", shift_perm(n, s))
        full = lax.dynamic_update_slice_in_dim(full, part, (c - s) % n * rows, axis=0)
    return full


def reduce_scatter_col(partial, send_dtype=jnp.float32):
    n = lax.axis_size("col")
    c = lax.axis_index("col")
    blocks = partial.reshape((n, -1) + partial.shape[1:])
    total = lax.dynamic_index_in_dim(blocks, c, axis=0, keepdims=False)
    for s in range(1, n):
        piece = lax.dynamic_index_in_dim(blocks, (c + s) % n, axis=0, keepdims=False)
        piece = lax.ppermute(piece.astype(send_dtype), "col", shift_perm(n, s))
        total = total + piece.astype(jnp.float32)
    return total


def body(activations, out_grad, gate_pre, up_proj, gate_weight, up_weight, down_weight):
    gate_float = gate_pre.astype(jnp.float32)
    up_float = up_proj.astype(jnp.float32)
    sigmoid_gate = jax.nn.sigmoid(gate_float)
    silu_gate = gate_float * sigmoid_gate
    hidden_local = (silu_gate * up_float).astype(jnp.bfloat16)
    hidden_act = lax.all_gather(hidden_local, ROW, axis=0, tiled=True)
    grad_full = gather_col(out_grad)
    activations, grad_full = lax.optimization_barrier((activations, grad_full))
    act_full = gather_col(activations)
    tokens_all = act_full.shape[0]
    chips = lax.axis_size("z")
    z = lax.axis_index("z")
    core = lax.axis_index("core")
    width = grad_full.shape[1]
    grad_blocks = grad_full.reshape(chips, 2, -1, width)
    grad_send = lax.dynamic_index_in_dim(grad_blocks, 1 - core, axis=1, keepdims=False)
    grad_keep = lax.dynamic_index_in_dim(grad_blocks, core, axis=1, keepdims=False)
    hid_send = lax.dot_general(
        grad_send.reshape(-1, width), down_weight, CONTRACT_LAST, preferred_element_type=jnp.float32
    )
    hid_recv = lax.ppermute(hid_send, "core", [(0, 1), (1, 0)])
    hid_keep = lax.dot_general(
        grad_keep.reshape(-1, width), down_weight, CONTRACT_LAST, preferred_element_type=jnp.float32
    )
    chip_sum = (hid_keep + hid_recv).reshape(chips, -1, hid_keep.shape[1])
    chip_sum, hidden_act, act_full = lax.optimization_barrier((chip_sum, hidden_act, act_full))
    hid_rows = lax.dynamic_index_in_dim(chip_sum, z, axis=0, keepdims=False)
    for s in [1] + list(range(chips - 1, 1, -1)):
        piece = lax.dynamic_index_in_dim(chip_sum, (z + s) % chips, axis=0, keepdims=False)
        piece = lax.ppermute(piece.astype(jnp.bfloat16), "z", shift_perm(chips, s))
        hid_rows = hid_rows + piece.astype(jnp.float32)
    gate_local = (
        hid_rows * up_float * sigmoid_gate * (1.0 + gate_float * (1.0 - sigmoid_gate))
    ).astype(jnp.bfloat16)
    gate_local, hid_rows = lax.optimization_barrier((gate_local, hid_rows))
    up_local = (hid_rows * silu_gate).astype(jnp.bfloat16)
    acc_down = lax.dot_general(
        hidden_act, grad_full, CONTRACT_FIRST, preferred_element_type=jnp.float32
    )
    gate_delta = lax.all_gather(gate_local, ROW, axis=0, tiled=True)
    up_delta = lax.all_gather(up_local, ROW, axis=0, tiled=True)
    acc_gate = lax.dot_general(
        act_full, gate_delta, CONTRACT_FIRST, preferred_element_type=jnp.float32
    )
    input_gate = reduce_scatter_col(
        lax.dot_general(gate_delta, gate_weight, CONTRACT_LAST, preferred_element_type=jnp.float32)
    )
    acc_gate, input_gate, up_delta = lax.optimization_barrier((acc_gate, input_gate, up_delta))
    input_up = lax.dot_general(
        up_delta, up_weight, CONTRACT_LAST, preferred_element_type=jnp.float32
    )
    up_delta, input_up = lax.optimization_barrier((up_delta, input_up))
    input_up = reduce_scatter_col(input_up, jnp.bfloat16)
    acc_up = lax.dot_general(act_full, up_delta, CONTRACT_FIRST, preferred_element_type=jnp.float32)
    input_rows = (input_gate + input_up).astype(jnp.bfloat16)
    factor = float(tokens_all) ** (-0.5)
    return (
        input_rows,
        (acc_gate * factor).astype(jnp.bfloat16),
        (acc_up * factor).astype(jnp.bfloat16),
        (acc_down * factor).astype(jnp.bfloat16),
    )


def solution(mesh):
    in_specs = (
        P("col", ROW),
        P("col", ROW),
        P(ROW, "col"),
        P(ROW, "col"),
        P(ROW, "col"),
        P(ROW, "col"),
        P("col", ROW),
    )
    out_specs = (P("col", ROW), P(ROW, "col"), P(ROW, "col"), P("col", ROW))
    devices = mesh.devices.reshape(mesh.shape["row"] // 2, 2, mesh.shape["col"])
    split_mesh = jax.sharding.Mesh(devices, ("z", "core", "col"))
    return jax.shard_map(
        body, mesh=split_mesh, in_specs=in_specs, out_specs=out_specs, check_vma=False
    )
```

profile of v0, /device:TPU:0, one launch (start us, length us, event | category | flops | bytes accessed | tf_op | source)
XLA Modules:
  0.0 409.8 jit_solution(13424678668484892783)
XLA Ops:
  7.2 0.0 all-gather.4.cloned.1.call-start
  7.2 3.2 fusion
  10.4 0.0 all-gather.4.cloned.1.call-update
  10.4 0.0 all-gather.6.cloned.1.call-start
  10.5 3.0 collective-permute-start
  13.5 1.5 collective-permute-start.1
  15.0 1.4 collective-permute-start.2
  16.4 0.3 broadcast.18.clone
  16.7 0.0 copy-start.2
  16.8 10.6 %collective-permute-done = bf16[256,1024]{1,0:T(8,128)(2,1)} collective-permute-done((bf16[256,1024]{1,0:T(8,128)(2,1)S(1)}, bf16[256,1024]{1,0:T(8,128)(2,1)}, u32[]{:S(2)}, u32[]{:S(2)}) %collective-permute-start) | collective-permute-done | bytes 524320 | tf_op jit(solution)/shard_map/ppermute | solution.py:22
  27.3 1.1 constant_dynamic-update-slice_fusion.6
  28.4 9.3 %collective-permute-done.1 = bf16[256,1024]{1,0:T(8,128)(2,1)} collective-permute-done((bf16[256,1024]{1,0:T(8,128)(2,1)S(1)}, bf16[256,1024]{1,0:T(8,128)(2,1)}, u32[]{:S(2)}, u32[]{:S(2)}) %collective-permute-start.1) | collective-permute-done | bytes 524320 | tf_op jit(solution)/shard_map/ppermute | solution.py:22
  37.7 1.1 constant_dynamic-update-slice_fusion.5
  38.8 0.0 collective-permute-done.2
  38.8 0.2 constant_dynamic-slice_fusion.1
  39.1 6.8 %fusion.23 = f32[512,4096]{1,0:T(8,128)} fusion(bf16[512,1024]{1,0:T(8,128)(2,1)S(1)} %bitcast.71, bf16[4096,1024]{1,0:T(8,128)(2,1)S(1)} %copy-done.2), kind=kOutput, calls=%fused_computation.54 | convolution fusion | flops 4294967296 | bytes 17825792 | tf_op jit(solution)/shard_map/dot_general | solution.py:57
  45.9 0.0 collective-permute-start.3
  45.9 2.0 collective-permute-start.4
  47.9 0.4 collective-permute-start.5
  48.3 2.3 collective-permute-start.6
  50.6 1.6 broadcast.18
  52.2 1.9 constant_dynamic-update-slice_fusion.3
  54.0 7.9 %collective-permute-done.4 = bf16[256,1024]{1,0:T(8,128)(2,1)} collective-permute-done((bf16[256,1024]{1,0:T(8,128)(2,1)}, bf16[256,1024]{1,0:T(8,128)(2,1)}, u32[]{:S(2)}, u32[]{:S(2)}) %collective-permute-start.4) | collective-permute-done | bytes 524320 | tf_op jit(solution)/shard_map/ppermute | solution.py:22
  61.9 1.9 constant_dynamic-update-slice_fusion.2
  63.8 8.9 %collective-permute-done.5 = bf16[256,1024]{1,0:T(8,128)(2,1)} collective-permute-done((bf16[256,1024]{1,0:T(8,128)(2,1)}, bf16[256,1024]{1,0:T(8,128)(2,1)}, u32[]{:S(2)}, u32[]{:S(2)}) %collective-permute-start.5) | collective-permute-done | bytes 524320 | tf_op jit(solution)/shard_map/ppermute | solution.py:22
  72.7 1.9 constant_dynamic-update-slice_fusion.1
  74.6 1.9 constant_dynamic-update-slice_fusion
  76.4 0.0 collective-permute-done.3
  76.4 11.5 %convolution_add_fusion = f32[512,4096]{1,0:T(8,128)} fusion(f32[512,4096]{1,0:T(8,128)} %collective-permute-done.3, bf16[512,1024]{1,0:T(8,128)(2,1)S(1)} %bitcast.70, bf16[4096,1024]{1,0:T(8,128)(2,1)} %param.13), kind=kOutput, calls=%fused_computation.3 | convolution fusion | flops 4297064448 | bytes 26214400 | tf_op jit(solution)/shard_map/dot_general | solution.py:61
  88.0 7.4 %all-gather.4.cloned.1.call-done = bf16[1024,4096]{1,0:T(8,128)(2,1)} async-done(((bf16[128,4096]{1,0:T(8,128)(2,1)}), bf16[1024,4096]{1,0:T(8,128)(2,1)}) %all-gather.4.cloned.1.call-update) | async-done | bytes 8388624 | tf_op jit(solution)/shard_map/all_gather | solution.py:45
  95.3 4.7 %fusion.10 = (bf16[128,4096]{1,0:T(8,128)(2,1)}, bf16[128,4096]{1,0:T(8,128)(2,1)}, bf16[128,4096]{1,0:T(8,128)(2,1)}) fusion(f32[4,128,4096]{2,1,0:T(8,128)} %bitcast.66, s32[]{:T(128)S(6)} %select_n.115, s32[]{:T(128)S(6)} %select_n.119, s32[]{:T(128)S(6)} %select_n.117), kind=kLoop, calls=%fused_computation.24 | loop fusion | bytes 6291468 | tf_op jit(solution)/shard_map/convert_element_type | solution.py:69
  100.1 0.0 collective-permute-start.7
  100.1 1.2 collective-permute-start.9
  101.2 2.7 collective-permute-start.8
  103.9 24.4 %collective-permute-done.7 = bf16[128,4096]{1,0:T(8,128)(2,1)} collective-permute-done((bf16[128,4096]{1,0:T(8,128)(2,1)}, bf16[128,4096]{1,0:T(8,128)(2,1)}, u32[]{:S(2)}, u32[]{:S(2)}) %collective-permute-start.7) | collective-permute-done | bytes 1048608 | tf_op jit(solution)/shard_map/ppermute | solution.py:69
  128.3 43.9 %collective-permute-done.9 = bf16[128,4096]{1,0:T(8,128)(2,1)} collective-permute-done((bf16[128,4096]{1,0:T(8,128)(2,1)}, bf16[128,4096]{1,0:T(8,128)(2,1)}, u32[]{:S(2)}, u32[]{:S(2)}) %collective-permute-start.9) | collective-permute-done | bytes 1048608 | tf_op jit(solution)/shard_map/ppermute | solution.py:69
  172.3 0.0 collective-permute-done.8
  172.3 5.8 %fusion.3 = (bf16[128,4096]{1,0:T(8,128)(2,1)}, f32[128,4096]{1,0:T(8,128)}) fusion(bf16[128,4096]{1,0:T(8,128)(2,1)} %param.10, bf16[128,4096]{1,0:T(8,128)(2,1)S(1)} %copy-done, bf16[128,4096]{1,0:T(8,128)(2,1)} %collective-permute-done.9, bf16[128,4096]{1,0:T(8,128)(2,1)} %collective-permute-done.8, bf16[128,4096]{1,0:T(8,128)(2,1)} %collective-permute-done.7, ...), kind=kLoop, calls=%fused_computation.12 | loop fusion | flops 9437184 | bytes 10485764 | tf_op jit(solution)/shard_map/convert_element_type | solution.py:73
  178.1 0.0 all-gather.6.cloned.1.call-update
  178.1 0.2 all-gather.8.cloned.1.call-start
  178.4 3.2 multiply_convert_fusion.3
  181.5 0.0 all-gather.8.cloned.1.call-update
  181.6 14.6 %multiply_convert_fusion = bf16[4096,1024]{1,0:T(8,128)(2,1)} fusion(bf16[1024,4096]{1,0:T(8,128)(2,1)} %all-gather.4.cloned.1.call-done, bf16[1024,1024]{1,0:T(8,128)(2,1)S(1)} %constant_dynamic-update-slice_fusion.4), kind=kOutput, calls=%fused_computation | convolution fusion | flops 8598323200 | bytes 18874368 | tf_op jit(solution)/shard_map/dot_general | solution.py:76
  196.2 84.4 %all-gather.6.cloned.1.call-done = bf16[1024,4096]{1,0:T(8,128)(2,1)} async-done(((bf16[128,4096]{1,0:T(8,128)(2,1)}), bf16[1024,4096]{1,0:T(8,128)(2,1)}) %all-gather.6.cloned.1.call-update) | async-done | bytes 8388624 | tf_op jit(solution)/shard_map/all_gather | solution.py:79
  280.6 12.8 %fusion.25 = f32[1024,1024]{1,0:T(8,128)S(1)} fusion(bf16[1024,4096]{1,0:T(8,128)(2,1)} %all-gather.6.cloned.1.call-done, bf16[1024,4096]{1,0:T(8,128)(2,1)} %param.11), kind=kOutput, calls=%fused_computation.56 | convolution fusion | flops 8589934592 | bytes 20971520 | tf_op jit(solution)/shard_map/dot_general | solution.py:85
  293.4 0.3 dynamic-slice_bitcast_fusion.2
  293.7 1.6 collective-permute-start.10
  295.3 1.4 collective-permute-start.12
  296.7 1.5 collective-permute-start.11
  298.2 13.7 %fusion.24 = f32[1024,4096]{1,0:T(8,128)} fusion(bf16[1024,1024]{1,0:T(8,128)(2,1)} %constant_dynamic-update-slice_fusion, bf16[1024,4096]{1,0:T(8,128)(2,1)S(1)} %copy-done.3), kind=kOutput, calls=%fused_computation.55 | convolution fusion | flops 8589934592 | bytes 27262976 | tf_op jit(solution)/shard_map/dot_general | solution.py:81
  311.9 8.8 %collective-permute-done.10 = f32[256,1024]{1,0:T(8,128)S(1)} collective-permute-done((f32[256,1024]{1,0:T(8,128)S(1)}, f32[256,1024]{1,0:T(8,128)S(1)}, u32[]{:S(2)}, u32[]{:S(2)}) %collective-permute-start.10) | collective-permute-done | bytes 1048608 | tf_op jit(solution)/shard_map/ppermute | solution.py:34
  320.7 21.8 %collective-permute-done.12 = f32[256,1024]{1,0:T(8,128)S(1)} collective-permute-done((f32[256,1024]{1,0:T(8,128)S(1)}, f32[256,1024]{1,0:T(8,128)S(1)}, u32[]{:S(2)}, u32[]{:S(2)}) %collective-permute-start.12) | collective-permute-done | bytes 1048608 | tf_op jit(solution)/shard_map/ppermute | solution.py:34
  342.5 0.0 collective-permute-done.11
  342.5 0.4 fusion.18
  342.9 19.9 %all-gather.8.cloned.1.call-done = bf16[1024,4096]{1,0:T(8,128)(2,1)} async-done(((bf16[128,4096]{1,0:T(8,128)(2,1)}), bf16[1024,4096]{1,0:T(8,128)(2,1)}) %all-gather.8.cloned.1.call-update) | async-done | bytes 8388624 | tf_op jit(solution)/shard_map/all_gather | solution.py:80
  362.8 12.6 %fusion.26 = f32[1024,1024]{1,0:T(8,128)S(1)} fusion(bf16[1024,4096]{1,0:T(8,128)(2,1)} %all-gather.8.cloned.1.call-done, bf16[1024,4096]{1,0:T(8,128)(2,1)} %param.12), kind=kOutput, calls=%fused_computation.57 | convolution fusion | flops 8589934592 | bytes 20971520 | tf_op jit(solution)/shard_map/dot_general | solution.py:88
  375.5 0.2 fusion.19
  375.8 1.6 collective-permute-start.13
  377.3 1.4 collective-permute-start.15
  378.7 1.5 collective-permute-start.14
  380.3 15.6 %multiply_convert_fusion.1 = bf16[1024,4096]{1,0:T(8,128)(2,1)} fusion(bf16[1024,1024]{1,0:T(8,128)(2,1)} %constant_dynamic-update-slice_fusion, bf16[1024,4096]{1,0:T(8,128)(2,1)} %all-gather.8.cloned.1.call-done), kind=kOutput, calls=%fused_computation.1 | convolution fusion | flops 8598323200 | bytes 18874368 | tf_op jit(solution)/shard_map/dot_general | solution.py:93
  395.9 4.0 multiply_convert_fusion.2
  399.9 2.2 collective-permute-done.15
  402.1 1.2 fusion.16
  (21 shorter events, 0.1 us)
Async XLA Ops:
  7.2 3.3 copy-start.1
  7.2 88.2 %all-gather.4.cloned.1.call-start = ((), (), s32[]{:S(2)}) async-start(), calls=%async_computation | async-start | bytes 9437184 | tf_op jit(solution)/shard_map/all_gather | solution.py:45
  10.4 270.2 %all-gather.6.cloned.1.call-start = ((), (), s32[]{:S(2)}) async-start(), calls=%async_computation.1 | async-start | bytes 9437184 | tf_op jit(solution)/shard_map/all_gather | solution.py:79
  10.5 16.8 %collective-permute-start = (bf16[256,1024]{1,0:T(8,128)(2,1)S(1)}, bf16[256,1024]{1,0:T(8,128)(2,1)}, u32[]{:S(2)}, u32[]{:S(2)}) collective-permute-start(bf16[256,1024]{1,0:T(8,128)(2,1)S(1)} %copy-done.1), channel_id=1, source_target_pairs={{0,1},{1,2},{2,3},{3,0},{4,5},{5,6},{6,7},{7,4},{8,9},{9,10},{10,1... | collective-permute-start | bytes 1572872 | tf_op jit(solution)/shard_map/ppermute | solution.py:22
  13.5 24.2 %collective-permute-start.1 = (bf16[256,1024]{1,0:T(8,128)(2,1)S(1)}, bf16[256,1024]{1,0:T(8,128)(2,1)}, u32[]{:S(2)}, u32[]{:S(2)}) collective-permute-start(bf16[256,1024]{1,0:T(8,128)(2,1)S(1)} %copy-done.1), channel_id=1, source_target_pairs={{0,2},{1,3},{2,0},{3,1},{4,6},{5,7},{6,4},{7,5},{8,10},{9,11},{10,... | collective-permute-start | bytes 1572872 | tf_op jit(solution)/shard_map/ppermute | solution.py:22
  15.0 23.8 %collective-permute-start.2 = (bf16[256,1024]{1,0:T(8,128)(2,1)S(1)}, bf16[256,1024]{1,0:T(8,128)(2,1)S(1)}, u32[]{:S(2)}, u32[]{:S(2)}) collective-permute-start(bf16[256,1024]{1,0:T(8,128)(2,1)S(1)} %copy-done.1), channel_id=1, source_target_pairs={{0,3},{1,0},{2,1},{3,2},{4,7},{5,4},{6,5},{7,6},{8,11},{9,8},{10,9... | collective-permute-start | bytes 1572872 | tf_op jit(solution)/shard_map/ppermute | solution.py:22
  16.7 22.4 %copy-start.2 = (bf16[4096,1024]{1,0:T(8,128)(2,1)S(1)}, bf16[4096,1024]{1,0:T(8,128)(2,1)}, u32[]{:S(2)}) copy-start(bf16[4096,1024]{1,0:T(8,128)(2,1)} %param.13) | copy-start | bytes 25165828
  45.9 30.5 %collective-permute-start.3 = (f32[512,4096]{1,0:T(8,128)}, f32[512,4096]{1,0:T(8,128)}, u32[]{:S(2)}, u32[]{:S(2)}) collective-permute-start(f32[512,4096]{1,0:T(8,128)} %fusion.23), channel_id=1, source_target_pairs={{0,4},{4,0},{1,5},{5,1},{2,6},{6,2},{3,7},{7,3},{8,12},{12,8},{9,1... | collective-permute-start | bytes 25165832 | tf_op jit(solution)/shard_map/ppermute | solution.py:60
  45.9 16.0 %collective-permute-start.4 = (bf16[256,1024]{1,0:T(8,128)(2,1)}, bf16[256,1024]{1,0:T(8,128)(2,1)}, u32[]{:S(2)}, u32[]{:S(2)}) collective-permute-start(bf16[256,1024]{1,0:T(8,128)(2,1)} %param.7), channel_id=1, source_target_pairs={{0,1},{1,2},{2,3},{3,0},{4,5},{5,6},{6,7},{7,4},{8,9},{9,10},{10,1... | collective-permute-start | bytes 1572872 | tf_op jit(solution)/shard_map/ppermute | solution.py:22
  47.9 24.8 %collective-permute-start.5 = (bf16[256,1024]{1,0:T(8,128)(2,1)}, bf16[256,1024]{1,0:T(8,128)(2,1)}, u32[]{:S(2)}, u32[]{:S(2)}) collective-permute-start(bf16[256,1024]{1,0:T(8,128)(2,1)} %param.7), channel_id=1, source_target_pairs={{0,2},{1,3},{2,0},{3,1},{4,6},{5,7},{6,4},{7,5},{8,10},{9,11},{10,... | collective-permute-start | bytes 1572872 | tf_op jit(solution)/shard_map/ppermute | solution.py:22
  48.3 26.3 %collective-permute-start.6 = (bf16[256,1024]{1,0:T(8,128)(2,1)}, bf16[256,1024]{1,0:T(8,128)(2,1)}, u32[]{:S(2)}, u32[]{:S(2)}) collective-permute-start(bf16[256,1024]{1,0:T(8,128)(2,1)} %param.7), channel_id=1, source_target_pairs={{0,3},{1,0},{2,1},{3,2},{4,7},{5,4},{6,5},{7,6},{8,11},{9,8},{10,9... | collective-permute-start | bytes 1572872 | tf_op jit(solution)/shard_map/ppermute | solution.py:22
  95.3 76.9 %copy-start = (bf16[128,4096]{1,0:T(8,128)(2,1)S(1)}, bf16[128,4096]{1,0:T(8,128)(2,1)}, u32[]{:S(2)}) copy-start(bf16[128,4096]{1,0:T(8,128)(2,1)} %param.9) | copy-start | bytes 3145732
  100.1 28.3 %collective-permute-start.7 = (bf16[128,4096]{1,0:T(8,128)(2,1)}, bf16[128,4096]{1,0:T(8,128)(2,1)}, u32[]{:S(2)}, u32[]{:S(2)}) collective-permute-start(bf16[128,4096]{1,0:T(8,128)(2,1)} %get-tuple-element.30), channel_id=1, source_target_pairs={{0,8},{8,16},{16,24},{24,0},{1,9},{9,17},{17,25},{25,1},{2,10},{10... | collective-permute-start | bytes 3145736 | tf_op jit(solution)/shard_map/ppermute | solution.py:69
  100.1 72.2 %collective-permute-start.9 = (bf16[128,4096]{1,0:T(8,128)(2,1)}, bf16[128,4096]{1,0:T(8,128)(2,1)}, u32[]{:S(2)}, u32[]{:S(2)}) collective-permute-start(bf16[128,4096]{1,0:T(8,128)(2,1)} %get-tuple-element.31), channel_id=1, source_target_pairs={{0,16},{8,24},{16,0},{24,8},{1,17},{9,25},{17,1},{25,9},{2,18},{10... | collective-permute-start | bytes 3145736 | tf_op jit(solution)/shard_map/ppermute | solution.py:69
  101.2 71.0 %collective-permute-start.8 = (bf16[128,4096]{1,0:T(8,128)(2,1)}, bf16[128,4096]{1,0:T(8,128)(2,1)}, u32[]{:S(2)}, u32[]{:S(2)}) collective-permute-start(bf16[128,4096]{1,0:T(8,128)(2,1)} %get-tuple-element.32), channel_id=1, source_target_pairs={{0,24},{8,0},{16,8},{24,16},{1,25},{9,1},{17,9},{25,17},{2,26},{10... | collective-permute-start | bytes 3145736 | tf_op jit(solution)/shard_map/ppermute | solution.py:69
  178.1 184.7 %all-gather.8.cloned.1.call-start = ((), (), s32[]{:S(2)}) async-start(), calls=%async_computation.2 | async-start | bytes 9437184 | tf_op jit(solution)/shard_map/all_gather | solution.py:80
  280.6 17.6 %copy-start.3 = (bf16[1024,4096]{1,0:T(8,128)(2,1)S(1)}, bf16[1024,4096]{1,0:T(8,128)(2,1)}, u32[]{:S(2)}) copy-start(bf16[1024,4096]{1,0:T(8,128)(2,1)} %all-gather.6.cloned.1.call-done) | copy-start | bytes 25165828
  293.7 27.0 %collective-permute-start.10 = (f32[256,1024]{1,0:T(8,128)S(1)}, f32[256,1024]{1,0:T(8,128)S(1)}, u32[]{:S(2)}, u32[]{:S(2)}) collective-permute-start(f32[256,1024]{1,0:T(8,128)S(1)} %get-tuple-element.36), channel_id=1, source_target_pairs={{0,1},{1,2},{2,3},{3,0},{4,5},{5,6},{6,7},{7,4},{8,9},{9,10},{10,1... | collective-permute-start | bytes 3145736 | tf_op jit(solution)/shard_map/ppermute | solution.py:34
  295.3 47.3 %collective-permute-start.12 = (f32[256,1024]{1,0:T(8,128)S(1)}, f32[256,1024]{1,0:T(8,128)S(1)}, u32[]{:S(2)}, u32[]{:S(2)}) collective-permute-start(f32[256,1024]{1,0:T(8,128)S(1)} %get-tuple-element.37), channel_id=1, source_target_pairs={{0,3},{1,0},{2,1},{3,2},{4,7},{5,4},{6,5},{7,6},{8,11},{9,8},{10,9... | collective-permute-start | bytes 3145736 | tf_op jit(solution)/shard_map/ppermute | solution.py:34
  296.7 45.9 %collective-permute-start.11 = (f32[256,1024]{1,0:T(8,128)S(1)}, f32[256,1024]{1,0:T(8,128)S(1)}, u32[]{:S(2)}, u32[]{:S(2)}) collective-permute-start(f32[256,1024]{1,0:T(8,128)S(1)} %get-tuple-element.38), channel_id=1, source_target_pairs={{0,2},{1,3},{2,0},{3,1},{4,6},{5,7},{6,4},{7,5},{8,10},{9,11},{10,... | collective-permute-start | bytes 3145736 | tf_op jit(solution)/shard_map/ppermute | solution.py:34
  375.5 20.3 %slice-start = ((s8[16777216]{0:T(1024)(128)(4,1)}), s8[4194304]{0:T(1024)(128)(4,1)S(1)}, s32[]{:S(2)}) async-start(s8[16777216]{0:T(1024)(128)(4,1)} %bitcast.61), calls=%async_computation.3 | async-start | bytes 8388608
  375.8 24.1 %collective-permute-start.13 = (bf16[256,1024]{1,0:T(8,128)(2,1)S(1)}, bf16[256,1024]{1,0:T(8,128)(2,1)S(1)}, u32[]{:S(2)}, u32[]{:S(2)}) collective-permute-start(bf16[256,1024]{1,0:T(8,128)(2,1)S(1)} %get-tuple-element.33), channel_id=1, source_target_pairs={{0,1},{1,2},{2,3},{3,0},{4,5},{5,6},{6,7},{7,4},{8,9},{9,10},{10,1... | collective-permute-start | bytes 1572872 | tf_op jit(solution)/shard_map/ppermute | solution.py:34
  377.3 24.8 %collective-permute-start.15 = (bf16[256,1024]{1,0:T(8,128)(2,1)S(1)}, bf16[256,1024]{1,0:T(8,128)(2,1)S(1)}, u32[]{:S(2)}, u32[]{:S(2)}) collective-permute-start(bf16[256,1024]{1,0:T(8,128)(2,1)S(1)} %get-tuple-element.34), channel_id=1, source_target_pairs={{0,3},{1,0},{2,1},{3,2},{4,7},{5,4},{6,5},{7,6},{8,11},{9,8},{10,9... | collective-permute-start | bytes 1572872 | tf_op jit(solution)/shard_map/ppermute | solution.py:34
  378.7 17.1 %slice-start.1 = ((s8[16777216]{0:T(1024)(128)(4,1)}), s8[4194304]{0:T(1024)(128)(4,1)S(1)}, s32[]{:S(2)}) async-start(s8[16777216]{0:T(1024)(128)(4,1)} %bitcast.61), calls=%async_computation.4 | async-start | bytes 8388608
  378.7 17.1 %slice-start.2 = ((s8[16777216]{0:T(1024)(128)(4,1)}), s8[4194304]{0:T(1024)(128)(4,1)S(1)}, s32[]{:S(2)}) async-start(s8[16777216]{0:T(1024)(128)(4,1)} %bitcast.61), calls=%async_computation.5 | async-start | bytes 8388608
  378.7 17.1 %slice-start.3 = ((s8[16777216]{0:T(1024)(128)(4,1)}), s8[4194304]{0:T(1024)(128)(4,1)S(1)}, s32[]{:S(2)}) async-start(s8[16777216]{0:T(1024)(128)(4,1)} %bitcast.61), calls=%async_computation.6 | async-start | bytes 8388608
  378.7 23.4 %collective-permute-start.14 = (bf16[256,1024]{1,0:T(8,128)(2,1)S(1)}, bf16[256,1024]{1,0:T(8,128)(2,1)S(1)}, u32[]{:S(2)}, u32[]{:S(2)}) collective-permute-start(bf16[256,1024]{1,0:T(8,128)(2,1)S(1)} %get-tuple-element.35), channel_id=1, source_target_pairs={{0,2},{1,3},{2,0},{3,1},{4,6},{5,7},{6,4},{7,5},{8,10},{9,11},{10,... | collective-permute-start | bytes 1572872 | tf_op jit(solution)/shard_map/ppermute | solution.py:34
Sparse Core Ops, SparseCore 0:
  10.6 84.7 all-gather.3
  178.2 102.3 all-gather.5
  282.2 80.5 all-gather.7
where the time goes:
time: 410 us
  waiting for transfers between devices  250 us (61%)
  matrix products  87.6 us (21%)
  starting transfers between devices  23.8 us (6%)
  other arithmetic  17.8 us (4%)
  local copies, waits for them, and re-layouts  17.1 us (4%)
  between operations  14 us (3%)
    all_gather x1, waiting for transfers between devices, body(): gate_delta = lax.all_gather(gate_local, ROW, axis=0, tiled=True)  84.4 us
    ppermute x3, waiting for transfers between devices, body(): piece = lax.ppermute(piece.astype(jnp.bfloat16), 'z', shift_perm(chips, s))  68.3 us
    ppermute x6, waiting for transfers between devices, gather_col(): part = lax.ppermute(block, 'col', shift_perm(n, s))  36.6 us
    ppermute x6, waiting for transfers between devices, reduce_scatter_col(): piece = lax.ppermute(piece.astype(send_dtype), 'col', shift_perm(n, s))  32.9 us
    all_gather x1, waiting for transfers between devices, body(): up_delta = lax.all_gather(up_local, ROW, axis=0, tiled=True)  19.9 us
    dot_general x1, matrix products, body(): lax.dot_general(act_full, up_delta, CONTRACT_FIRST, preferred_element_typ...  15.6 us
    dot_general x1, matrix products, body(): lax.dot_general(hidden_act, grad_full, CONTRACT_FIRST, preferred_element_...  14.6 us
    dot_general x1, matrix products, body(): lax.dot_general(act_full, gate_delta, CONTRACT_FIRST, preferred_element_t...  13.7 us
  transfers between devices with their start and end apart: 19, of which 12 were waited for; matrix products, arithmetic and copies ran while one was open for 23% of the time, Pallas kernels for 0%

commit v1 on v0

--- a/solution.py
+++ b/solution.py
@@ -2,6 +2,7 @@
 import jax.numpy as jnp
 from jax import lax
 from jax.sharding import PartitionSpec as P
+from jax.lax import all_gather
 
 CONTRACT_LAST = (((1,), (1,)), ((), ()))
 CONTRACT_FIRST = (((0,), (0,)), ((), ()))
@@ -76,8 +77,12 @@
     acc_down = lax.dot_general(
         hidden_act, grad_full, CONTRACT_FIRST, preferred_element_type=jnp.float32
     )
-    gate_delta = lax.all_gather(gate_local, ROW, axis=0, tiled=True)
-    up_delta = lax.all_gather(up_local, ROW, axis=0, tiled=True)
+
+    def launch_task_for(array_in, base_x):
+        work_now = jnp.concatenate([array_in, base_x], axis=1)
+        return jnp.split(all_gather(work_now, ROW, axis=0, tiled=True), [array_in.shape[1]], 1)
+
+    gate_delta, up_delta = launch_task_for(gate_local, up_local)
     acc_gate = lax.dot_general(
         act_full, gate_delta, CONTRACT_FIRST, preferred_element_type=jnp.float32
     )

time: 410 us -> 464 us (1.13)
  waiting for transfers between devices: 250 us -> 296 us
  local copies, waits for them, and re-layouts: 17.1 us -> 27.2 us
    all_gather x2 -> x1, waiting for transfers between devices: 104 us -> 157 us  [launch_task_for(): all_gather(work_now, ROW, axis=0, tiled=True)]
    split x0 -> x1, local copies, waits for them, and re-layouts: none -> 7.89 us  [launch_task_for(): jnp.split(all_gather(work_now, ROW, axis=0, tiled=True), [array_in.shape[...]
    ppermute x6, waiting for transfers between devices: 32.9 us -> 27.1 us  [reduce_scatter_col(): piece = lax.ppermute(piece.astype(send_dtype), 'col', shift_perm(n, s))]
  transfers between devices with their start and end apart: 19 -> 18, of which waited for: 12 -> 11; matrix products, arithmetic and copies ran while one was open for 23% -> 18% of each run, Pallas kernels for 0% -> 0%
where the time goes in v1:
time: 464 us; the launch traced here: 463 us
  waiting for transfers between devices  296 us (64%)
  matrix products  85.5 us (18%)
  local copies, waits for them, and re-layouts  27.2 us (6%)
  starting transfers between devices  23.4 us (5%)
  other arithmetic  16.5 us (4%)
  between operations  14.2 us (3%)
    all_gather x1, waiting for transfers between devices, launch_task_for(): all_gather(work_now, ROW, axis=0, tiled=True)  157 us
    ppermute x3, waiting for transfers between devices, body(): piece = lax.ppermute(piece.astype(jnp.bfloat16), 'z', shift_perm(chips, s))  68.3 us
    ppermute x6, waiting for transfers between devices, gather_col(): part = lax.ppermute(block, 'col', shift_perm(n, s))  36.4 us
    ppermute x6, waiting for transfers between devices, reduce_scatter_col(): piece = lax.ppermute(piece.astype(send_dtype), 'col', shift_perm(n, s))  27.1 us
    dot_general x1, matrix products, body(): lax.dot_general(act_full, up_delta, CONTRACT_FIRST, preferred_element_typ...  14.9 us
    dot_general x1, matrix products, body(): lax.dot_general(hidden_act, grad_full, CONTRACT_FIRST, preferred_element_...  14.6 us
    dot_general x1, matrix products, body(): lax.dot_general(gate_delta, gate_weight, CONTRACT_LAST, preferred_element...  12.7 us
    dot_general x1, matrix products, body(): lax.dot_general(up_delta, up_weight, CONTRACT_LAST, preferred_element_typ...  12.6 us
  transfers between devices with their start and end apart: 18, of which 11 were waited for; matrix products, arithmetic and copies ran while one was open for 18% of the time, Pallas kernels for 0%

profile of v1, /device:TPU:0, one launch (start us, length us, event | category | flops | bytes accessed | tf_op | source)
XLA Modules:
  0.0 463.1 jit_solution(10371404103566476740)
XLA Ops:
  7.2 0.0 all-gather.3.cloned.1.call-start
  7.2 3.2 fusion.4
  10.4 0.0 all-gather.3.cloned.1.call-update
  10.4 0.0 all-gather.5.cloned.1.call-start
  10.5 3.0 collective-permute-start
  13.5 1.5 collective-permute-start.1
  15.0 1.4 collective-permute-start.2
  16.4 0.3 broadcast.18.clone
  16.7 0.0 copy-start.3
  16.8 10.6 %collective-permute-done = bf16[256,1024]{1,0:T(8,128)(2,1)} collective-permute-done((bf16[256,1024]{1,0:T(8,128)(2,1)S(1)}, bf16[256,1024]{1,0:T(8,128)(2,1)}, u32[]{:S(2)}, u32[]{:S(2)}) %collective-permute-start) | collective-permute-done | bytes 524320 | tf_op jit(solution)/shard_map/ppermute | solution.py:23
  27.3 1.1 constant_dynamic-update-slice_fusion.6
  28.4 9.3 %collective-permute-done.1 = bf16[256,1024]{1,0:T(8,128)(2,1)} collective-permute-done((bf16[256,1024]{1,0:T(8,128)(2,1)S(1)}, bf16[256,1024]{1,0:T(8,128)(2,1)}, u32[]{:S(2)}, u32[]{:S(2)}) %collective-permute-start.1) | collective-permute-done | bytes 524320 | tf_op jit(solution)/shard_map/ppermute | solution.py:23
  37.7 1.1 constant_dynamic-update-slice_fusion.5
  38.8 0.0 collective-permute-done.2
  38.8 0.2 constant_dynamic-slice_fusion.1
  39.1 6.8 %fusion.27 = f32[512,4096]{1,0:T(8,128)} fusion(bf16[512,1024]{1,0:T(8,128)(2,1)S(1)} %bitcast.67, bf16[4096,1024]{1,0:T(8,128)(2,1)S(1)} %copy-done.3), kind=kOutput, calls=%fused_computation.59 | convolution fusion | flops 4294967296 | bytes 17825792 | tf_op jit(solution)/shard_map/dot_general | solution.py:58
  45.9 0.0 collective-permute-start.3
  45.9 2.0 collective-permute-start.4
  47.9 0.4 collective-permute-start.5
  48.3 2.3 collective-permute-start.6
  50.6 1.6 broadcast.18
  52.2 2.0 constant_dynamic-update-slice_fusion.3
  54.2 7.7 %collective-permute-done.4 = bf16[256,1024]{1,0:T(8,128)(2,1)} collective-permute-done((bf16[256,1024]{1,0:T(8,128)(2,1)}, bf16[256,1024]{1,0:T(8,128)(2,1)}, u32[]{:S(2)}, u32[]{:S(2)}) %collective-permute-start.4) | collective-permute-done | bytes 524320 | tf_op jit(solution)/shard_map/ppermute | solution.py:23
  61.9 1.9 constant_dynamic-update-slice_fusion.2
  63.8 8.9 %collective-permute-done.5 = bf16[256,1024]{1,0:T(8,128)(2,1)} collective-permute-done((bf16[256,1024]{1,0:T(8,128)(2,1)}, bf16[256,1024]{1,0:T(8,128)(2,1)}, u32[]{:S(2)}, u32[]{:S(2)}) %collective-permute-start.5) | collective-permute-done | bytes 524320 | tf_op jit(solution)/shard_map/ppermute | solution.py:23
  72.7 1.9 constant_dynamic-update-slice_fusion.1
  74.6 0.0 collective-permute-done.6
  74.6 1.9 constant_dynamic-update-slice_fusion
  76.4 11.5 %convolution_add_fusion = f32[512,4096]{1,0:T(8,128)} fusion(f32[512,4096]{1,0:T(8,128)} %collective-permute-done.3, bf16[512,1024]{1,0:T(8,128)(2,1)S(1)} %bitcast.66, bf16[4096,1024]{1,0:T(8,128)(2,1)} %param.13), kind=kOutput, calls=%fused_computation.7 | convolution fusion | flops 4297064448 | bytes 26214400 | tf_op jit(solution)/shard_map/dot_general | solution.py:62
  88.0 7.4 %all-gather.3.cloned.1.call-done = bf16[1024,4096]{1,0:T(8,128)(2,1)} async-done(((bf16[128,4096]{1,0:T(8,128)(2,1)}), bf16[1024,4096]{1,0:T(8,128)(2,1)}) %all-gather.3.cloned.1.call-update) | async-done | bytes 8388624 | tf_op jit(solution)/shard_map/all_gather | solution.py:46
  95.3 4.7 %fusion.14 = (bf16[128,4096]{1,0:T(8,128)(2,1)}, bf16[128,4096]{1,0:T(8,128)(2,1)}, bf16[128,4096]{1,0:T(8,128)(2,1)}) fusion(f32[4,128,4096]{2,1,0:T(8,128)} %bitcast.62, s32[]{:T(128)S(6)} %select_n.115, s32[]{:T(128)S(6)} %select_n.119, s32[]{:T(128)S(6)} %select_n.117), kind=kLoop, calls=%fused_computation.29 | loop fusion | bytes 6291468 | tf_op jit(solution)/shard_map/convert_element_type | solution.py:70
  100.1 0.0 collective-permute-start.7
  100.1 1.2 collective-permute-start.9
  101.3 2.7 collective-permute-start.8
  104.0 24.4 %collective-permute-done.7 = bf16[128,4096]{1,0:T(8,128)(2,1)} collective-permute-done((bf16[128,4096]{1,0:T(8,128)(2,1)}, bf16[128,4096]{1,0:T(8,128)(2,1)}, u32[]{:S(2)}, u32[]{:S(2)}) %collective-permute-start.7) | collective-permute-done | bytes 1048608 | tf_op jit(solution)/shard_map/ppermute | solution.py:70
  128.4 43.9 %collective-permute-done.9 = bf16[128,4096]{1,0:T(8,128)(2,1)} collective-permute-done((bf16[128,4096]{1,0:T(8,128)(2,1)}, bf16[128,4096]{1,0:T(8,128)(2,1)}, u32[]{:S(2)}, u32[]{:S(2)}) %collective-permute-start.9) | collective-permute-done | bytes 1048608 | tf_op jit(solution)/shard_map/ppermute | solution.py:70
  172.3 4.2 fusion.7
  176.5 0.6 multiply_convert_fusion.3
  177.1 1.5 pad_maximum_fusion
  178.5 0.0 all-gather.5.cloned.1.call-update
  178.6 14.6 %multiply_convert_fusion = bf16[4096,1024]{1,0:T(8,128)(2,1)} fusion(bf16[1024,4096]{1,0:T(8,128)(2,1)} %all-gather.3.cloned.1.call-done, bf16[1024,1024]{1,0:T(8,128)(2,1)S(1)} %constant_dynamic-update-slice_fusion.4), kind=kOutput, calls=%fused_computation | convolution fusion | flops 8598323200 | bytes 18874368 | tf_op jit(solution)/shard_map/dot_general | solution.py:77
  193.2 156.9 %all-gather.5.cloned.1.call-done = bf16[1024,8192]{1,0:T(8,128)(2,1)} async-done(((bf16[128,8192]{1,0:T(8,128)(2,1)}), bf16[1024,8192]{1,0:T(8,128)(2,1)}) %all-gather.5.cloned.1.call-update) | async-done | bytes 16777232 | tf_op jit(solution)/shard_map/all_gather | solution.py:83
  350.1 12.7 %fusion = f32[1024,1024]{1,0:T(8,128)S(1)} fusion(bf16[1024,4096]{1,0:T(8,128)(2,1)} %param.11, bf16[1024,8192]{1,0:T(8,128)(2,1)} %all-gather.5.cloned.1.call-done), kind=kOutput, calls=%fused_computation.3 | convolution fusion | flops 8589934592 | bytes 20971520 | tf_op jit(solution)/shard_map/dot_general | solution.py:90
  362.8 0.0 copy-start.1
  362.8 1.5 dynamic-slice_bitcast_fusion.2
  364.3 0.9 copy-done.1
  365.1 1.5 collective-permute-start.10
  366.6 1.5 collective-permute-start.12
  368.1 1.5 collective-permute-start.11
  369.5 7.9 %split.9 = bf16[1024,4096]{1,0:T(8,128)(2,1)} slice(bf16[1024,8192]{1,0:T(8,128)(2,1)} %all-gather.5.cloned.1.call-done), slice={[0:1024], [4096:8192]} | slice | bytes 16777216 | tf_op jit(solution)/shard_map/split | solution.py:83
  377.4 12.4 %fusion.2 = f32[1024,4096]{1,0:T(8,128)S(1)} fusion(bf16[1024,1024]{1,0:T(8,128)(2,1)} %constant_dynamic-update-slice_fusion, bf16[1024,8192]{1,0:T(8,128)(2,1)} %all-gather.5.cloned.1.call-done), kind=kOutput, calls=%fused_computation.5 | convolution fusion | flops 8589934592 | bytes 27262976 | tf_op jit(solution)/shard_map/dot_general | solution.py:86
  389.8 2.5 collective-permute-done.10
  392.3 21.8 %collective-permute-done.12 = f32[256,1024]{1,0:T(8,128)S(1)} collective-permute-done((f32[256,1024]{1,0:T(8,128)S(1)}, f32[256,1024]{1,0:T(8,128)S(1)}, u32[]{:S(2)}, u32[]{:S(2)}) %collective-permute-start.12) | collective-permute-done | bytes 1048608 | tf_op jit(solution)/shard_map/ppermute | solution.py:35
  414.1 0.0 collective-permute-done.11
  414.1 1.9 fusion.22
  416.1 12.6 %fusion.28 = f32[1024,1024]{1,0:T(8,128)S(1)} fusion(bf16[1024,4096]{1,0:T(8,128)(2,1)} %split.9, bf16[1024,4096]{1,0:T(8,128)(2,1)} %param.12), kind=kOutput, calls=%fused_computation.60 | convolution fusion | flops 8589934592 | bytes 20971520 | tf_op jit(solution)/shard_map/dot_general | solution.py:93
  428.7 0.2 fusion.23
  429.0 1.9 collective-permute-start.13
  430.9 1.2 collective-permute-start.15
  432.1 1.3 collective-permute-start.14
  433.4 14.9 %multiply_convert_fusion.1 = bf16[1024,4096]{1,0:T(8,128)(2,1)} fusion(bf16[1024,1024]{1,0:T(8,128)(2,1)} %constant_dynamic-update-slice_fusion, bf16[1024,4096]{1,0:T(8,128)(2,1)} %split.9), kind=kOutput, calls=%fused_computation.1 | convolution fusion | flops 8598323200 | bytes 18874368 | tf_op jit(solution)/shard_map/dot_general | solution.py:98
  448.4 4.0 multiply_convert_fusion.2
  452.3 2.8 collective-permute-done.15
  455.1 1.2 fusion.20
  (11 shorter events, 0.1 us)
Async XLA Ops:
  7.2 3.3 copy-start.2
  7.2 88.2 %all-gather.3.cloned.1.call-start = ((), (), s32[]{:S(2)}) async-start(), calls=%async_computation | async-start | bytes 9437184 | tf_op jit(solution)/shard_map/all_gather | solution.py:46
  10.4 339.7 %all-gather.5.cloned.1.call-start = ((), (), s32[]{:S(2)}) async-start(), calls=%async_computation.1 | async-start | bytes 18874368 | tf_op jit(solution)/shard_map/all_gather | solution.py:83
  10.5 16.8 %collective-permute-start = (bf16[256,1024]{1,0:T(8,128)(2,1)S(1)}, bf16[256,1024]{1,0:T(8,128)(2,1)}, u32[]{:S(2)}, u32[]{:S(2)}) collective-permute-start(bf16[256,1024]{1,0:T(8,128)(2,1)S(1)} %copy-done.2), channel_id=1, source_target_pairs={{0,1},{1,2},{2,3},{3,0},{4,5},{5,6},{6,7},{7,4},{8,9},{9,10},{10,1... | collective-permute-start | bytes 1572872 | tf_op jit(solution)/shard_map/ppermute | solution.py:23
  13.5 24.2 %collective-permute-start.1 = (bf16[256,1024]{1,0:T(8,128)(2,1)S(1)}, bf16[256,1024]{1,0:T(8,128)(2,1)}, u32[]{:S(2)}, u32[]{:S(2)}) collective-permute-start(bf16[256,1024]{1,0:T(8,128)(2,1)S(1)} %copy-done.2), channel_id=1, source_target_pairs={{0,2},{1,3},{2,0},{3,1},{4,6},{5,7},{6,4},{7,5},{8,10},{9,11},{10,... | collective-permute-start | bytes 1572872 | tf_op jit(solution)/shard_map/ppermute | solution.py:23
  15.0 23.8 %collective-permute-start.2 = (bf16[256,1024]{1,0:T(8,128)(2,1)S(1)}, bf16[256,1024]{1,0:T(8,128)(2,1)S(1)}, u32[]{:S(2)}, u32[]{:S(2)}) collective-permute-start(bf16[256,1024]{1,0:T(8,128)(2,1)S(1)} %copy-done.2), channel_id=1, source_target_pairs={{0,3},{1,0},{2,1},{3,2},{4,7},{5,4},{6,5},{7,6},{8,11},{9,8},{10,9... | collective-permute-start | bytes 1572872 | tf_op jit(solution)/shard_map/ppermute | solution.py:23
  16.7 22.4 %copy-start.3 = (bf16[4096,1024]{1,0:T(8,128)(2,1)S(1)}, bf16[4096,1024]{1,0:T(8,128)(2,1)}, u32[]{:S(2)}) copy-start(bf16[4096,1024]{1,0:T(8,128)(2,1)} %param.13) | copy-start | bytes 25165828
  45.9 30.5 %collective-permute-start.3 = (f32[512,4096]{1,0:T(8,128)}, f32[512,4096]{1,0:T(8,128)}, u32[]{:S(2)}, u32[]{:S(2)}) collective-permute-start(f32[512,4096]{1,0:T(8,128)} %fusion.27), channel_id=1, source_target_pairs={{0,4},{4,0},{1,5},{5,1},{2,6},{6,2},{3,7},{7,3},{8,12},{12,8},{9,1... | collective-permute-start | bytes 25165832 | tf_op jit(solution)/shard_map/ppermute | solution.py:61
  45.9 16.0 %collective-permute-start.4 = (bf16[256,1024]{1,0:T(8,128)(2,1)}, bf16[256,1024]{1,0:T(8,128)(2,1)}, u32[]{:S(2)}, u32[]{:S(2)}) collective-permute-start(bf16[256,1024]{1,0:T(8,128)(2,1)} %param.7), channel_id=1, source_target_pairs={{0,1},{1,2},{2,3},{3,0},{4,5},{5,6},{6,7},{7,4},{8,9},{9,10},{10,1... | collective-permute-start | bytes 1572872 | tf_op jit(solution)/shard_map/ppermute | solution.py:23
  47.9 24.8 %collective-permute-start.5 = (bf16[256,1024]{1,0:T(8,128)(2,1)}, bf16[256,1024]{1,0:T(8,128)(2,1)}, u32[]{:S(2)}, u32[]{:S(2)}) collective-permute-start(bf16[256,1024]{1,0:T(8,128)(2,1)} %param.7), channel_id=1, source_target_pairs={{0,2},{1,3},{2,0},{3,1},{4,6},{5,7},{6,4},{7,5},{8,10},{9,11},{10,... | collective-permute-start | bytes 1572872 | tf_op jit(solution)/shard_map/ppermute | solution.py:23
  48.3 26.3 %collective-permute-start.6 = (bf16[256,1024]{1,0:T(8,128)(2,1)}, bf16[256,1024]{1,0:T(8,128)(2,1)}, u32[]{:S(2)}, u32[]{:S(2)}) collective-permute-start(bf16[256,1024]{1,0:T(8,128)(2,1)} %param.7), channel_id=1, source_target_pairs={{0,3},{1,0},{2,1},{3,2},{4,7},{5,4},{6,5},{7,6},{8,11},{9,8},{10,9... | collective-permute-start | bytes 1572872 | tf_op jit(solution)/shard_map/ppermute | solution.py:23
  95.3 77.0 %copy-start = (bf16[128,4096]{1,0:T(8,128)(2,1)S(1)}, bf16[128,4096]{1,0:T(8,128)(2,1)}, u32[]{:S(2)}) copy-start(bf16[128,4096]{1,0:T(8,128)(2,1)} %param.9) | copy-start | bytes 3145732
  100.1 28.3 %collective-permute-start.7 = (bf16[128,4096]{1,0:T(8,128)(2,1)}, bf16[128,4096]{1,0:T(8,128)(2,1)}, u32[]{:S(2)}, u32[]{:S(2)}) collective-permute-start(bf16[128,4096]{1,0:T(8,128)(2,1)} %get-tuple-element.30), channel_id=1, source_target_pairs={{0,8},{8,16},{16,24},{24,0},{1,9},{9,17},{17,25},{25,1},{2,10},{10... | collective-permute-start | bytes 3145736 | tf_op jit(solution)/shard_map/ppermute | solution.py:70
  100.1 72.2 %collective-permute-start.9 = (bf16[128,4096]{1,0:T(8,128)(2,1)}, bf16[128,4096]{1,0:T(8,128)(2,1)}, u32[]{:S(2)}, u32[]{:S(2)}) collective-permute-start(bf16[128,4096]{1,0:T(8,128)(2,1)} %get-tuple-element.31), channel_id=1, source_target_pairs={{0,16},{8,24},{16,0},{24,8},{1,17},{9,25},{17,1},{25,9},{2,18},{10... | collective-permute-start | bytes 3145736 | tf_op jit(solution)/shard_map/ppermute | solution.py:70
  101.3 71.0 %collective-permute-start.8 = (bf16[128,4096]{1,0:T(8,128)(2,1)}, bf16[128,4096]{1,0:T(8,128)(2,1)}, u32[]{:S(2)}, u32[]{:S(2)}) collective-permute-start(bf16[128,4096]{1,0:T(8,128)(2,1)} %get-tuple-element.32), channel_id=1, source_target_pairs={{0,24},{8,0},{16,8},{24,16},{1,25},{9,1},{17,9},{25,17},{2,26},{10... | collective-permute-start | bytes 3145736 | tf_op jit(solution)/shard_map/ppermute | solution.py:70
  362.8 2.3 copy-start.1
  365.1 27.1 %collective-permute-start.10 = (f32[256,1024]{1,0:T(8,128)}, f32[256,1024]{1,0:T(8,128)S(1)}, u32[]{:S(2)}, u32[]{:S(2)}) collective-permute-start(f32[256,1024]{1,0:T(8,128)} %get-tuple-element.36), channel_id=1, source_target_pairs={{0,1},{1,2},{2,3},{3,0},{4,5},{5,6},{6,7},{7,4},{8,9},{9,10},{10,1... | collective-permute-start | bytes 3145736 | tf_op jit(solution)/shard_map/ppermute | solution.py:35
  366.6 47.5 %collective-permute-start.12 = (f32[256,1024]{1,0:T(8,128)S(1)}, f32[256,1024]{1,0:T(8,128)S(1)}, u32[]{:S(2)}, u32[]{:S(2)}) collective-permute-start(f32[256,1024]{1,0:T(8,128)S(1)} %get-tuple-element.37), channel_id=1, source_target_pairs={{0,3},{1,0},{2,1},{3,2},{4,7},{5,4},{6,5},{7,6},{8,11},{9,8},{10,9... | collective-permute-start | bytes 3145736 | tf_op jit(solution)/shard_map/ppermute | solution.py:35
  368.1 46.1 %collective-permute-start.11 = (f32[256,1024]{1,0:T(8,128)S(1)}, f32[256,1024]{1,0:T(8,128)}, u32[]{:S(2)}, u32[]{:S(2)}) collective-permute-start(f32[256,1024]{1,0:T(8,128)S(1)} %get-tuple-element.38), channel_id=1, source_target_pairs={{0,2},{1,3},{2,0},{3,1},{4,6},{5,7},{6,4},{7,5},{8,10},{9,11},{10,... | collective-permute-start | bytes 3145736 | tf_op jit(solution)/shard_map/ppermute | solution.py:35
  429.0 23.4 %collective-permute-start.13 = (bf16[256,1024]{1,0:T(8,128)(2,1)S(1)}, bf16[256,1024]{1,0:T(8,128)(2,1)S(1)}, u32[]{:S(2)}, u32[]{:S(2)}) collective-permute-start(bf16[256,1024]{1,0:T(8,128)(2,1)S(1)} %get-tuple-element.33), channel_id=1, source_target_pairs={{0,1},{1,2},{2,3},{3,0},{4,5},{5,6},{6,7},{7,4},{8,9},{9,10},{10,1... | collective-permute-start | bytes 1572872 | tf_op jit(solution)/shard_map/ppermute | solution.py:35
  430.9 24.2 %collective-permute-start.15 = (bf16[256,1024]{1,0:T(8,128)(2,1)S(1)}, bf16[256,1024]{1,0:T(8,128)(2,1)S(1)}, u32[]{:S(2)}, u32[]{:S(2)}) collective-permute-start(bf16[256,1024]{1,0:T(8,128)(2,1)S(1)} %get-tuple-element.34), channel_id=1, source_target_pairs={{0,3},{1,0},{2,1},{3,2},{4,7},{5,4},{6,5},{7,6},{8,11},{9,8},{10,9... | collective-permute-start | bytes 1572872 | tf_op jit(solution)/shard_map/ppermute | solution.py:35
  432.1 23.0 %collective-permute-start.14 = (bf16[256,1024]{1,0:T(8,128)(2,1)S(1)}, bf16[256,1024]{1,0:T(8,128)(2,1)S(1)}, u32[]{:S(2)}, u32[]{:S(2)}) collective-permute-start(bf16[256,1024]{1,0:T(8,128)(2,1)S(1)} %get-tuple-element.35), channel_id=1, source_target_pairs={{0,2},{1,3},{2,0},{3,1},{4,6},{5,7},{6,4},{7,5},{8,10},{9,11},{10,... | collective-permute-start | bytes 1572872 | tf_op jit(solution)/shard_map/ppermute | solution.py:35
Sparse Core Ops, SparseCore 0:
  10.6 84.7 all-gather.2
  178.7 171.3 all-gather.4
